TPU v7x, 128 devices: a whole 4x4x4 slice. The times are simulated.
128 devices in a mesh: tm: 32 (over x, z, core), feat: 4 (over y).
Axes of the slice: x: 4, y: 4, z: 4, core: 2. Of those that a mesh axis runs over, the one named last changes fastest.
Arguments:
- activations: bfloat16 [81920, 2048], P(('tm', 'feat')), may hold values from -19 to 19
- targets: bfloat16 [81920, 128], P(('tm', 'feat')), may hold values from -8 to 8
- span_of: int32 [81920], P(('tm', 'feat')), may hold values from 0 to 31, as said below
Outputs:
- predictions: bfloat16 [81920, 128], P(('tm', 'feat'))
- surprise: float32 [81920], P(('tm', 'feat'))
Inputs may be any that keep to these rules, and one draw needn't show every extreme that they name: `span_of`: in each aligned block of 640 rows (the rows of one device) every span from 0 to 31 appears exactly 20 times.
All inputs are finite; a program needn't handle non-finite values.
Results may differ from a plain program's by a relative error of at most 0.0049.
Values may be sent and summed in bfloat16 or wider, within the bound.
No kernel may reach another device: no remote copies, remote signals or barrier semaphores. Data moves between devices by JAX's collectives and lax.ppermute only.
A program may use at most 320 MiB of HBM per device.

v0:
```python
import jax
import jax.numpy as jnp
from jax import lax
from jax.sharding import PartitionSpec as P

ITERS = 3
RIDGE = 0.1
TINY = 1e-06


def carried_in(shard, axis, combine, identity):
    length, position = (lax.axis_size(axis), lax.axis_index(axis))
    everything = jax.tree.map(lambda part: lax.all_gather(part, axis), shard)
    start = jax.tree.map(
        lambda part, zero: jnp.broadcast_to(jnp.asarray(zero, part.dtype), part.shape),
        shard,
        identity,
    )

    def hop(k, before):
        reached = k < position
        new = combine(before, jax.tree.map(lambda part: part[k], everything))
        return jax.tree.map(lambda a, b: jnp.where(reached, a, b), new, before)

    return lax.fori_loop(0, length, hop, start)


def body(activations, targets, span_of):
    spans = lax.axis_size("tm")
    feat_count = lax.axis_size("feat")
    tok_dev, width = activations.shape
    n_targets = targets.shape[1]
    block_rows = width // feat_count
    share = tok_dev // spans
    contract = (((0,), (0,)), ((), ()))
    highest = lax.Precision.HIGHEST
    order = jnp.argsort(span_of, stable=True)
    sorted_x = jnp.take(activations, order, axis=0).reshape(spans, share, width)
    sorted_y = jnp.take(targets, order, axis=0).reshape(spans, share, n_targets)
    moved_x, moved_y = (
        lax.all_to_all(sorted_x, "tm", split_axis=0, concat_axis=0, tiled=True),
        lax.all_to_all(sorted_y, "tm", split_axis=0, concat_axis=0, tiled=True),
    )
    local_x = moved_x.reshape(tok_dev, width)
    local_y = moved_y.reshape(tok_dev, n_targets)
    col_start = lax.axis_index("feat") * block_rows
    rows_x = lax.all_gather(local_x, "feat", axis=0, tiled=True)
    rows_y = lax.all_gather(local_y, "feat", axis=0, tiled=True)
    own = lax.dynamic_slice_in_dim(rows_x, col_start, block_rows, 1)
    gram_part = lax.dot_general(own, rows_x, contract, preferred_element_type=jnp.float32)
    cross_part = lax.dot_general(own, rows_y, contract, preferred_element_type=jnp.float32)

    def combine(earlier, later):
        return (earlier[0] + later[0], earlier[1] + later[1])

    identity = (jnp.zeros_like(gram_part), jnp.zeros_like(cross_part))
    gram_prefix, cross_prefix = carried_in((gram_part, cross_part), "tm", combine, identity)
    seen = (lax.axis_index("tm") * (tok_dev * feat_count)).astype(jnp.float32)
    scale = 1.0 / jnp.maximum(seen, 1.0)
    rhs = scale * cross_prefix

    def column_dot(left, right):
        return lax.psum(jnp.sum(left * right, axis=0), "feat")

    residual = rhs
    direction = rhs
    norm_now = column_dot(residual, residual)
    solution = None
    for step in range(ITERS):
        product = jnp.dot(
            gram_prefix,
            lax.all_gather(direction, "feat", axis=0, tiled=True),
            precision=highest,
            preferred_element_type=jnp.float32,
        )
        product, carried = (product, direction)
        image = scale * product + RIDGE * direction
        alpha = norm_now / (column_dot(direction, image) + TINY)
        update = alpha * carried
        solution = update if solution is None else solution + update
        if step + 1 < ITERS:
            residual = residual - alpha * image
            norm_next = column_dot(residual, residual)
            direction = residual + norm_next / (norm_now + TINY) * direction
            norm_now = norm_next
    weights = lax.all_gather(solution.astype(jnp.bfloat16), "feat", axis=0, tiled=True)
    predicted = jnp.dot(local_x, weights, preferred_element_type=jnp.float32).astype(jnp.bfloat16)
    returned = lax.all_to_all(
        predicted.reshape(spans, share, n_targets), "tm", split_axis=0, concat_axis=0, tiled=True
    )
    in_order = returned.reshape(tok_dev, n_targets)
    predictions = jnp.zeros_like(in_order).at[order].set(in_order)
    error = targets.astype(jnp.float32) - predictions.astype(jnp.float32)
    surprise = jnp.mean(error * error, axis=1)
    return (predictions, surprise)


def solution(mesh):
    return jax.shard_map(
        body,
        mesh=mesh,
        in_specs=(P(("tm", "feat"), None), P(("tm", "feat"), None), P(("tm", "feat"))),
        out_specs=(P(("tm", "feat"), None), P(("tm", "feat"))),
        check_vma=False,
    )
```

profile of v0, /device:TPU:1, one launch (start us, length us, event | category | flops | bytes accessed | tf_op | source)
XLA Modules:
  0.0 1049.8 jit_solution(8673995626986290233)
XLA Ops:
  7.2 5.2 sort.17
  12.5 4.1 gather_fusion
  16.6 5.2 gather.13
  21.9 2.2 broadcast_select_fusion
  24.1 48.7 %all_to_all.15 = bf16[32,20,2048]{2,1,0:T(8,128)(2,1)} all-to-all(bf16[32,20,2048]{2,1,0:T(8,128)(2,1)S(1)} %broadcast_select_fusion), channel_id=1, replica_groups=mesh['tm'=32,'feat'=4] {'tm'}, dimensions={0} | all-to-all | bytes 5242880 | tf_op jit(solution)/shard_map/all_to_all | solution.py:41
  72.8 5.2 reshape.39
  78.1 2.0 gather_fusion.1
  81.0 3.9 all-to-all-start.1
  85.0 8.2 all-to-all-done.1
  93.9 16.8 %all_gather.33 = bf16[2560,128]{1,0:T(8,128)(2,1)S(1)} all-gather(bf16[640,128]{1,0:T(8,128)(2,1)} %reshape.40), channel_id=1, replica_groups=mesh['tm'=32,'feat'=4] {'feat'}, dimensions={0}, use_global_device_ids=true | all-gather | bytes 819200 | tf_op jit(solution)/shard_map/all_gather | solution.py:48
  110.7 71.1 %all-gather.9.cloned.1.call-done = bf16[2560,2048]{1,0:T(8,128)(2,1)} async-done(((bf16[640,2048]{1,0:T(8,128)(2,1)}), bf16[2560,2048]{1,0:T(8,128)(2,1)}) %all-gather.9.cloned.1.call-update) | async-done | bytes 10485776 | tf_op jit(solution)/shard_map/all_gather | solution.py:47
  181.8 3.3 fusion
  185.2 10.5 fusion.2
  195.8 43.9 %all-gather.19.cloned.1.call-done = f32[16384,128]{1,0:T(8,128)} async-done(((f32[512,128]{1,0:T(8,128)}), f32[16384,128]{1,0:T(8,128)}) %all-gather.19.cloned.1.call-update) | async-done | bytes 8388624 | tf_op jit(solution)/shard_map/all_gather | solution.py:13
  239.7 377.4 %all-gather.17.cloned.1.call-done = f32[16384,2048]{1,0:T(8,128)} async-done(((f32[512,2048]{1,0:T(8,128)}), f32[16384,2048]{1,0:T(8,128)}) %all-gather.17.cloned.1.call-update) | async-done | bytes 134217744 | tf_op jit(solution)/shard_map/all_gather | solution.py:13
  617.2 248.0 %while.16 = (s32[]{:T(128)}, f32[512,2048]{1,0:T(8,128)}, f32[512,128]{1,0:T(8,128)S(1)}, s32[]{:T(128)}, f32[32,512,2048]{2,1,0:T(8,128)}, /*index=5*/f32[32,512,128]{2,1,0:T(8,128)}, s32[]{:T(128)}, s32[]{:T(128)}) while((s32[]{:T(128)}, f32[512,2048]{1,0:T(8,128)}, f32[512,128]{1,0:T(8,128)S(1)}, s32[]{:T(128)}, ...), condition=%wide.region_2.3_spmd.clone, body=%wide.region_1.2_spmd.clone.sunk | while | flops 3342340 | bytes 13369459 | solution.py:25
  617.2 5.5 add_select_fusion.4
  623.7 6.7 add_select_fusion.4
  631.5 6.7 add_select_fusion.4
  639.2 6.7 add_select_fusion.4
  647.0 6.7 add_select_fusion.4
  654.8 6.7 add_select_fusion.4
  662.6 6.7 add_select_fusion.4
  670.4 6.7 add_select_fusion.4
  678.2 6.7 add_select_fusion.4
  686.0 6.7 add_select_fusion.4
  693.8 6.7 add_select_fusion.4
  701.6 6.7 add_select_fusion.4
  709.4 6.7 add_select_fusion.4
  717.1 6.7 add_select_fusion.4
  724.9 6.7 add_select_fusion.4
  732.7 6.7 add_select_fusion.4
  740.5 6.7 add_select_fusion.4
  748.3 6.7 add_select_fusion.4
  756.1 6.7 add_select_fusion.4
  763.9 6.7 add_select_fusion.4
  771.7 6.7 add_select_fusion.4
  779.5 6.7 add_select_fusion.4
  787.3 6.7 add_select_fusion.4
  795.0 6.7 add_select_fusion.4
  802.8 6.7 add_select_fusion.4
  810.6 6.7 add_select_fusion.4
  818.4 6.7 add_select_fusion.4
  826.2 6.7 add_select_fusion.4
  834.0 6.7 add_select_fusion.4
  841.8 6.7 add_select_fusion.4
  849.6 6.7 add_select_fusion.4
  857.4 6.7 add_select_fusion.4
  866.0 20.6 %all-gather.11.cloned.1.call-done = f32[2048,128]{1,0:T(8,128)} async-done(((f32[512,128]{1,0:T(8,128)}), f32[2048,128]{1,0:T(8,128)}) %all-gather.11.cloned.1.call-update) | async-done | bytes 1048592 | tf_op jit(solution)/shard_map/all_gather | solution.py:72
  886.6 6.6 multiply_reduce_fusion.4
  893.2 7.8 all-reduce
  902.1 6.0 psum.44
  908.9 27.8 %all-gather.13.cloned.1.call-done = f32[2048,128]{1,0:T(8,128)} async-done(((f32[512,128]{1,0:T(8,128)}), f32[2048,128]{1,0:T(8,128)}) %all-gather.13.cloned.1.call-update) | async-done | bytes 1048592 | tf_op jit(solution)/shard_map/all_gather | solution.py:72
  936.7 6.6 multiply_reduce_fusion.2
  943.4 7.7 psum.45
  952.1 6.0 psum.46
  958.2 1.8 multiply_add_fusion
  960.0 27.8 %all-gather.15.cloned.1.call-done = f32[2048,128]{1,0:T(8,128)} async-done(((f32[512,128]{1,0:T(8,128)}), f32[2048,128]{1,0:T(8,128)}) %all-gather.15.cloned.1.call-update) | async-done | bytes 1048592 | tf_op jit(solution)/shard_map/all_gather | solution.py:72
  987.8 5.9 fusion.8
  993.7 7.7 psum.47
  1002.5 10.6 %all_gather.39 = bf16[2048,128]{1,0:T(8,128)(2,1)S(1)} all-gather(bf16[512,128]{1,0:T(8,128)(2,1)S(1)} %add_convert_fusion), channel_id=1, replica_groups=mesh['tm'=32,'feat'=4] {'feat'}, dimensions={0}, use_global_device_ids=true | all-gather | bytes 655360 | tf_op jit(solution)/shard_map/all_gather | solution.py:86
  1013.1 2.6 convolution_convert_fusion
  1015.7 22.1 %all_to_all.16 = bf16[32,20,128]{2,1,0:T(8,128)(2,1)S(1)} all-to-all(bf16[32,20,128]{2,1,0:T(8,128)(2,1)S(1)} %reshape.41), channel_id=1, replica_groups=mesh['tm'=32,'feat'=4] {'tm'}, dimensions={0} | all-to-all | bytes 327680 | tf_op jit(solution)/shard_map/all_to_all | solution.py:88
  1037.9 4.3 scatter_custom_fusion
  (78 shorter events, 40.3 us)
Async XLA Ops:
  7.2 5.3 copy-start
  7.2 174.6 %all-gather.9.cloned.1.call-start = ((), (), s32[]{:S(2)}) async-start(), calls=%async_computation.3 | async-start | bytes 13107200 | tf_op jit(solution)/shard_map/all_gather | solution.py:47
  72.8 5.3 copy-start.1
  81.0 12.2 %all-to-all-start.1 = ((bf16[32,20,128]{2,1,0:T(8,128)(2,1)}), bf16[32,20,128]{2,1,0:T(8,128)(2,1)S(1)}, u32[]{:S(2)}, u32[]{:S(2)}) async-start(bf16[32,20,128]{2,1,0:T(8,128)(2,1)} %broadcast_select_fusion.1), calls=%async_computation.1 | async-start | bytes 393216 | tf_op jit(solution)/shard_map/all_to_all | solution.py:42
  84.9 154.8 %all-gather.19.cloned.1.call-start = ((), (), s32[]{:S(2)}) async-start(), calls=%async_computation.8 | async-start | bytes 8650752 | tf_op jit(solution)/shard_map/all_gather | solution.py:13
  185.2 432.0 %all-gather.17.cloned.1.call-start = ((), (), s32[]{:S(2)}) async-start(), calls=%async_computation.7 | async-start | bytes 138412032 | tf_op jit(solution)/shard_map/all_gather | solution.py:13
  195.7 690.9 %all-gather.11.cloned.1.call-start = ((), (), s32[]{:S(2)}) async-start(), calls=%async_computation.4 | async-start | bytes 1310720 | tf_op jit(solution)/shard_map/all_gather | solution.py:72
  865.9 70.8 %all-gather.13.cloned.1.call-start = ((), (), s32[]{:S(2)}) async-start(), calls=%async_computation.5 | async-start | bytes 1310720 | tf_op jit(solution)/shard_map/all_gather | solution.py:72
  902.1 6.0 copy-start.3
  908.9 49.3 %copy-start.2 = (f32[512,128]{1,0:T(8,128)S(1)}, f32[512,128]{1,0:T(8,128)}, u32[]{:S(2)}) copy-start(f32[512,128]{1,0:T(8,128)} %multiply_add_fusion.1) | copy-start | bytes 786436
  908.9 78.9 %all-gather.15.cloned.1.call-start = ((), (), s32[]{:S(2)}) async-start(), calls=%async_computation.6 | async-start | bytes 1310720 | tf_op jit(solution)/shard_map/all_gather | solution.py:72
  1042.2 0.8 copy-start.4
Sparse Core Ops, SparseCore 0:
  78.2 103.5 all-gather.8
  185.3 54.3 all-gather.18
  242.0 375.1 all-gather.16
  866.0 20.4 all-gather.10
  909.0 27.6 all-gather.12
  960.1 27.6 all-gather.14
where the time goes:
time: 1050 us
  waiting for transfers between devices  577 us (55%)
  other arithmetic  263 us (25%)
  blocking collectives  133 us (13%)
  matrix products  35.6 us (3%)
  local copies, waits for them, and re-layouts  21.7 us (2%)
  between operations  14.3 us (1%)
    all_gather x2, waiting for transfers between devices, carried_in(): everything = jax.tree.map(lambda part: lax.all_gather(part, axis), shard)  421 us
    select_n x64, other arithmetic, hop(): return jax.tree.map(lambda a, b: jnp.where(reached, a, b), new, before)  247 us
    all_gather x3, waiting for transfers between devices, body(): lax.all_gather(direction, 'feat', axis=0, tiled=True)  76.2 us
    all_gather x1, waiting for transfers between devices, body(): rows_x = lax.all_gather(local_x, 'feat', axis=0, tiled=True)  71.1 us
    all_to_all x1, blocking collectives, body(): lax.all_to_all(sorted_x, 'tm', split_axis=0, concat_axis=0, tiled=True)  48.7 us
    psum x5, blocking collectives, column_dot(): return lax.psum(jnp.sum(left * right, axis=0), 'feat')  35.2 us
    all_to_all x1, blocking collectives, body(): lax.all_to_all(predicted.reshape(spans, share, n_targets), 'tm', split_ax...  22.1 us
  transfers between devices with their start and end apart: 7, of which 7 were waited for; matrix products, arithmetic and copies ran while one was open for 1% of the time, Pallas kernels for 0%

commit v1 on v0

--- a/solution.py
+++ b/solution.py
@@ -6,6 +6,28 @@
 ITERS = 3
 RIDGE = 0.1
 TINY = 1e-06
+
+
+def joined_along(blocks, dim):
+    shape = list(blocks.shape[1:])
+    shape[dim] *= blocks.shape[0]
+    return jnp.moveaxis(blocks, 0, dim).reshape(shape)
+
+
+def gather_around(x, axis, dim):
+    size = lax.axis_size(axis)
+    pairs = [(i, (i + 1) % size) for i in range(size)]
+    back = [(b, a) for a, b in pairs]
+    lower, upper = ([], [])
+    for lap in range(size - 1):
+        if lap % 2 == 0:
+            lower.append(lax.ppermute(lower[-1] if lower else x, axis, pairs))
+        else:
+            upper.append(lax.ppermute(upper[-1] if upper else x, axis, back))
+    pieces = jnp.stack([*lower[::-1], x, *upper])
+    shift = lax.axis_index(axis) - len(lower)
+    pieces = pieces[(jnp.arange(size) - shift) % size]
+    return joined_along(pieces, dim)
 
 
 def carried_in(shard, axis, combine, identity):
@@ -69,7 +91,7 @@
     for step in range(ITERS):
         product = jnp.dot(
             gram_prefix,
-            lax.all_gather(direction, "feat", axis=0, tiled=True),
+            gather_around(direction, "feat", 0),
             precision=highest,
             preferred_element_type=jnp.float32,
         )

time: 1050 us -> 1040 us (level)
  waiting for transfers between devices: 577 us -> 538 us
    all_gather x3 -> x0, waiting for transfers between devices: 76.2 us -> none  [body(): lax.all_gather(direction, 'feat', axis=0, tiled=True)]
    ppermute x0 -> x9, waiting for transfers between devices: none -> 37.3 us  [the longest x6 37.3 us: gather_around(): lower.append(lax.ppermute(lower[-1] if lower else x, axis, pairs))]
  transfers between devices with their start and end apart: 7 -> 13, of which waited for: 7 -> 10; matrix products, arithmetic and copies ran while one was open for 1% -> 1% of each run, Pallas kernels for 0% -> 0%
where the time goes in v1:
time: 1040 us
  waiting for transfers between devices  538 us (52%)
  other arithmetic  266 us (26%)
  blocking collectives  140 us (13%)
  matrix products  34.5 us (3%)
  local copies, waits for them, and re-layouts  30.2 us (3%)
  between operations  14 us (1%)
  starting transfers between devices  12.5 us (1%)
    all_gather x2, waiting for transfers between devices, carried_in(): everything = jax.tree.map(lambda part: lax.all_gather(part, axis), shard)  421 us
    select_n x64, other arithmetic, hop(): return jax.tree.map(lambda a, b: jnp.where(reached, a, b), new, before)  247 us
    all_gather x1, waiting for transfers between devices, body(): rows_x = lax.all_gather(local_x, 'feat', axis=0, tiled=True)  71.1 us
    all_to_all x1, blocking collectives, body(): lax.all_to_all(sorted_x, 'tm', split_axis=0, concat_axis=0, tiled=True)  48.7 us
    ppermute x6, waiting for transfers between devices, gather_around(): lower.append(lax.ppermute(lower[-1] if lower else x, axis, pairs))  37.3 us
    psum x5, blocking collectives, column_dot(): return lax.psum(jnp.sum(left * right, axis=0), 'feat')  33.1 us
    all_to_all x1, blocking collectives, body(): lax.all_to_all(predicted.reshape(spans, share, n_targets), 'tm', split_ax...  31.7 us
  transfers between devices with their start and end apart: 13, of which 10 were waited for; matrix products, arithmetic and copies ran while one was open for 1% of the time, Pallas kernels for 0%

profile of v1, /device:TPU:1, one launch (start us, length us, event | category | flops | bytes accessed | tf_op | source)
XLA Modules:
  0.0 1035.9 jit_solution(3006205834173817658)
XLA Ops:
  7.2 5.2 sort.17
  12.5 4.1 gather_fusion
  16.6 5.2 gather.22
  24.1 48.7 %all_to_all.15 = bf16[32,20,2048]{2,1,0:T(8,128)(2,1)} all-to-all(bf16[32,20,2048]{2,1,0:T(8,128)(2,1)S(1)} %broadcast_select_fusion), channel_id=1, replica_groups=mesh['tm'=32,'feat'=4] {'tm'}, dimensions={0} | all-to-all | bytes 5242880 | tf_op jit(solution)/shard_map/all_to_all | solution.py:63
  72.8 5.2 reshape.97
  81.0 3.9 all-to-all-start.1
  85.0 8.2 all-to-all-done.1
  93.9 16.8 %all_gather.24 = bf16[2560,128]{1,0:T(8,128)(2,1)S(1)} all-gather(bf16[640,128]{1,0:T(8,128)(2,1)} %reshape.98), channel_id=1, replica_groups=mesh['tm'=32,'feat'=4] {'feat'}, dimensions={0}, use_global_device_ids=true | all-gather | bytes 819200 | tf_op jit(solution)/shard_map/all_gather | solution.py:70
  110.7 71.1 %all-gather.6.cloned.1.call-done = bf16[2560,2048]{1,0:T(8,128)(2,1)} async-done(((bf16[640,2048]{1,0:T(8,128)(2,1)}), bf16[2560,2048]{1,0:T(8,128)(2,1)}) %all-gather.6.cloned.1.call-update) | async-done | bytes 10485776 | tf_op jit(solution)/shard_map/all_gather | solution.py:69
  181.8 3.3 fusion
  185.2 10.5 %fusion.2 = f32[512,2048]{1,0:T(8,128)} fusion(bf16[2560,2048]{1,0:T(8,128)(2,1)} %all-gather.6.cloned.1.call-done, s32[]{:T(128)S(6)} %select_n.91), kind=kOutput, calls=%fused_computation.11 | convolution fusion | flops 5368709120 | bytes 17301508 | tf_op jit(solution)/shard_map/dot_general | solution.py:72
  195.8 43.9 %all-gather.10.cloned.1.call-done = f32[16384,128]{1,0:T(8,128)} async-done(((f32[512,128]{1,0:T(8,128)}), f32[16384,128]{1,0:T(8,128)}) %all-gather.10.cloned.1.call-update) | async-done | bytes 8388624 | tf_op jit(solution)/shard_map/all_gather | solution.py:35
  239.7 377.4 %all-gather.8.cloned.1.call-done = f32[16384,2048]{1,0:T(8,128)} async-done(((f32[512,2048]{1,0:T(8,128)}), f32[16384,2048]{1,0:T(8,128)}) %all-gather.8.cloned.1.call-update) | async-done | bytes 134217744 | tf_op jit(solution)/shard_map/all_gather | solution.py:35
  617.2 248.0 %while.16 = (s32[]{:T(128)}, f32[512,2048]{1,0:T(8,128)}, f32[512,128]{1,0:T(8,128)S(1)}, s32[]{:T(128)}, f32[32,512,2048]{2,1,0:T(8,128)}, /*index=5*/f32[32,512,128]{2,1,0:T(8,128)}, s32[]{:T(128)}, s32[]{:T(128)}) while((s32[]{:T(128)}, f32[512,2048]{1,0:T(8,128)}, f32[512,128]{1,0:T(8,128)S(1)}, s32[]{:T(128)}, ...), condition=%wide.region_2.3_spmd.clone, body=%wide.region_1.2_spmd.clone.sunk | while | flops 3342340 | bytes 13369459 | solution.py:47
  617.2 5.5 add_select_fusion.4
  623.7 6.7 add_select_fusion.4
  631.5 6.7 add_select_fusion.4
  639.2 6.7 add_select_fusion.4
  647.0 6.7 add_select_fusion.4
  654.8 6.7 add_select_fusion.4
  662.6 6.7 add_select_fusion.4
  670.4 6.7 add_select_fusion.4
  678.2 6.7 add_select_fusion.4
  686.0 6.7 add_select_fusion.4
  693.8 6.7 add_select_fusion.4
  701.6 6.7 add_select_fusion.4
  709.4 6.7 add_select_fusion.4
  717.1 6.7 add_select_fusion.4
  724.9 6.7 add_select_fusion.4
  732.7 6.7 add_select_fusion.4
  740.5 6.7 add_select_fusion.4
  748.3 6.7 add_select_fusion.4
  756.1 6.7 add_select_fusion.4
  763.9 6.7 add_select_fusion.4
  771.7 6.7 add_select_fusion.4
  779.5 6.7 add_select_fusion.4
  787.3 6.7 add_select_fusion.4
  795.0 6.7 add_select_fusion.4
  802.8 6.7 add_select_fusion.4
  810.6 6.7 add_select_fusion.4
  818.4 6.7 add_select_fusion.4
  826.2 6.7 add_select_fusion.4
  834.0 6.7 add_select_fusion.4
  841.8 6.7 add_select_fusion.4
  849.6 6.7 add_select_fusion.4
  857.4 6.7 add_select_fusion.4
  868.0 6.2 collective-permute-done
  874.2 8.1 collective-permute-done.1
  884.3 2.9 gather_fusion.2
  887.2 5.5 multiply_reduce_fusion.4
  892.7 6.0 all-reduce
  899.5 7.7 psum.44
  911.1 3.8 collective-permute-done.3
  915.0 9.0 collective-permute-done.4
  927.9 6.6 multiply_reduce_fusion.2
  934.5 6.0 psum.45
  941.6 7.4 psum.46
  952.9 3.8 collective-permute-done.6
  956.7 6.5 collective-permute-done.7
  967.1 6.0 fusion.8
  973.0 6.0 psum.47
  980.1 9.9 all_gather.27
  992.6 31.7 %all_to_all.16 = bf16[32,20,128]{2,1,0:T(8,128)(2,1)S(1)} all-to-all(bf16[32,20,128]{2,1,0:T(8,128)(2,1)S(1)} %reshape.102), channel_id=1, replica_groups=mesh['tm'=32,'feat'=4] {'tm'}, dimensions={0} | all-to-all | bytes 327680 | tf_op jit(solution)/shard_map/all_to_all | solution.py:110
  1024.3 4.3 scatter_custom_fusion
  (94 shorter events, 65.7 us)
Async XLA Ops:
  7.2 5.3 copy-start
  7.2 174.6 %all-gather.6.cloned.1.call-start = ((), (), s32[]{:S(2)}) async-start(), calls=%async_computation.3 | async-start | bytes 13107200 | tf_op jit(solution)/shard_map/all_gather | solution.py:69
  72.8 5.3 copy-start.1
  81.0 12.2 %all-to-all-start.1 = ((bf16[32,20,128]{2,1,0:T(8,128)(2,1)}), bf16[32,20,128]{2,1,0:T(8,128)(2,1)S(1)}, u32[]{:S(2)}, u32[]{:S(2)}) async-start(bf16[32,20,128]{2,1,0:T(8,128)(2,1)} %broadcast_select_fusion.1), calls=%async_computation.1 | async-start | bytes 393216 | tf_op jit(solution)/shard_map/all_to_all | solution.py:64
  84.9 154.8 %all-gather.10.cloned.1.call-start = ((), (), s32[]{:S(2)}) async-start(), calls=%async_computation.5 | async-start | bytes 8650752 | tf_op jit(solution)/shard_map/all_gather | solution.py:35
  185.2 432.0 %all-gather.8.cloned.1.call-start = ((), (), s32[]{:S(2)}) async-start(), calls=%async_computation.4 | async-start | bytes 138412032 | tf_op jit(solution)/shard_map/all_gather | solution.py:35
  865.2 9.0 collective-permute-start
  866.5 7.7 collective-permute-start.2
  874.2 8.2 collective-permute-start.1
  908.2 6.7 collective-permute-start.3
  908.5 6.5 collective-permute-start.5
  914.9 9.0 collective-permute-start.4
  950.2 13.0 %copy-start.2 = (f32[512,128]{1,0:T(8,128)}, f32[512,128]{1,0:T(8,128)S(1)}, u32[]{:S(2)}) copy-start(f32[512,128]{1,0:T(8,128)S(1)} %multiply_add_fusion) | copy-start | bytes 786436
  950.2 6.5 collective-permute-start.6
  950.3 6.4 collective-permute-start.8
  956.7 6.5 collective-permute-start.7
  1028.6 0.8 copy-start.3
Sparse Core Ops, SparseCore 0:
  78.2 103.5 all-gather.5
  185.3 54.3 all-gather.9
  242.0 375.1 all-gather.7
